TPU v7x, 128 devices: a whole 4x4x4 slice. The times are simulated.
128 devices in a mesh: sec: 4 (over z_hi, core), pts: 32 (over x, z_lo, y).
Axes of the slice: x: 4, y: 4, z: 4 (z_hi: 2, z_lo: 2; z = z_hi * 2 + z_lo), core: 2. Of those that a mesh axis runs over, the one named last changes fastest.
Arguments:
- points: bfloat16 [4, 32768, 1024], P('sec', 'pts'), may hold values from -10 to 10
- counts: int32 [4, 32], P('sec', 'pts'), may hold values from 256 to 1024, as said below
- input_gain: float32 [4, 1024], P('sec'), may hold values from 0.1 to 1.9
- key_weight: bfloat16 [4, 1024, 1024], P('sec', 'pts'), may hold values from -0.375 to 0.375
- value_weight: bfloat16 [4, 1024, 1024], P('sec', 'pts'), may hold values from -0.375 to 0.375
- query_weight: bfloat16 [1024, 1024], replicated, may hold values from -0.1875 to 0.1875
- output_weight: bfloat16 [1024, 1024], replicated, may hold values from -0.75 to 0.75
- middle_gain: float32 [1024], replicated, may hold values from 0.1 to 1.9
- up_weight: bfloat16 [1024, 4096], P(None, 'sec'), may hold values from -0.1875 to 0.1875
- down_weight: bfloat16 [4096, 1024], P('sec'), may hold values from -0.09375 to 0.09375
Outputs:
- updated: bfloat16 [32768, 1024], P('pts', 'sec')
Inputs may be any that keep to these rules, and one draw needn't show every extreme that they name: `counts`: each block has 1024 slots; in every section some block is full.
All inputs are finite; a program needn't handle non-finite values.
Results may differ from a plain program's by a relative error of at most 0.0049.
Values may be sent and summed in bfloat16 or wider, within the bound.
No kernel may reach another device: no remote copies, remote signals or barrier semaphores. Data moves between devices by JAX's collectives and lax.ppermute only.
A program may use at most 128 MiB of HBM per device.

v0:
```python
import jax
import jax.numpy as jnp
from jax import lax
from jax.sharding import PartitionSpec as P

HEAD_DIM = 128


def broadcast(value, axis, root):
    mine = lax.axis_index(axis) == root
    return lax.psum(jnp.where(mine, value, jnp.zeros_like(value)), axis)


def layer_normalizer(values, gain):
    mean = jnp.mean(values, axis=-1, keepdims=True)
    centred = values - mean
    spread = jnp.mean(centred * centred, axis=-1, keepdims=True)
    return centred * lax.rsqrt(spread + 1e-05) * gain


def feature_map(values):
    return jax.nn.elu(values) + 1.0


def on_device(
    points,
    counts,
    input_gain,
    key_weight,
    value_weight,
    query_weight,
    output_weight,
    middle_gain,
    up_weight,
    down_weight,
):
    block = points[0]
    rows = block.shape[0]
    width = block.shape[1]
    heads = width // HEAD_DIM
    sections = lax.axis_size("sec")
    normed = layer_normalizer(block.astype(jnp.float32), input_gain[0]).astype(jnp.bfloat16)

    def add_rows(piece):
        return jnp.dot(normed, piece[0], preferred_element_type=jnp.float32)

    summed_keys = add_rows(lax.all_gather(key_weight, "pts", axis=1, tiled=True))
    value_sums = add_rows(lax.all_gather(value_weight, "pts", axis=1, tiled=True))
    valid = jnp.arange(rows) < counts[0, 0]
    key_feats = feature_map(summed_keys).astype(jnp.bfloat16)
    key_feats = jnp.where(valid[:, None], key_feats, jnp.zeros_like(key_feats))
    value_rows = value_sums.astype(jnp.bfloat16)
    local_state = jnp.einsum(
        "yzl,yzn->zln",
        key_feats.reshape(rows, heads, HEAD_DIM),
        value_rows.reshape(rows, heads, HEAD_DIM),
        preferred_element_type=jnp.float32,
    ).reshape(width, HEAD_DIM)
    local_total = jnp.sum(key_feats.astype(jnp.float32), axis=0)
    part_state, part_total = (
        lax.all_gather(local_state[None], "sec", axis=0, tiled=True),
        lax.all_gather(local_total[None], "sec", axis=0, tiled=True),
    )
    state_matrices, totals = lax.psum((part_state, part_total), "pts")
    query_feats = feature_map(
        jnp.dot(normed, query_weight, preferred_element_type=jnp.float32)
    ).astype(jnp.bfloat16)
    query_feats = lax.optimization_barrier(query_feats)
    per_head_queries = query_feats.astype(jnp.float32).reshape(rows, heads, HEAD_DIM)
    state_heads = state_matrices.reshape(sections, heads, HEAD_DIM, HEAD_DIM)
    total_heads = totals.reshape(sections, heads, HEAD_DIM)
    numerator = jnp.einsum(
        "rhk,shkv->srhv", per_head_queries, state_heads, precision=lax.Precision.HIGHEST
    )
    denom = jnp.einsum(
        "rhk,shk->srh", per_head_queries, total_heads, precision=lax.Precision.HIGHEST
    )
    attended = (
        jnp.sum(numerator / denom[:, :, :, None], axis=0).reshape(rows, width).astype(jnp.bfloat16)
    )
    mixed = block.astype(jnp.float32) + jnp.dot(
        attended, output_weight, preferred_element_type=jnp.float32
    )
    centred = layer_normalizer(mixed, middle_gain).astype(jnp.bfloat16)
    shared = broadcast(centred, "sec", sections - 1)
    hidden = jax.nn.gelu(
        jnp.dot(shared, up_weight, preferred_element_type=jnp.float32), approximate=True
    ).astype(jnp.bfloat16)
    is_query = (lax.axis_index("sec") == sections - 1).astype(jnp.float32)
    term = jnp.dot(hidden, down_weight, preferred_element_type=jnp.float32) + is_query * mixed
    return lax.psum_scatter(term, "sec", scatter_dimension=1, tiled=True).astype(jnp.bfloat16)


def solution(mesh):
    placed = (
        P("sec", "pts", None),
        P("sec", "pts"),
        P("sec", None),
        P("sec", "pts", None),
        P("sec", "pts", None),
        P(),
        P(),
        P(),
        P(None, "sec"),
        P("sec", None),
    )
    return jax.shard_map(
        on_device, mesh=mesh, in_specs=placed, out_specs=P("pts", "sec"), check_vma=False
    )
```

profile of v0, /device:TPU:1, one launch (start us, length us, event | category | flops | bytes accessed | tf_op | source)
XLA Modules:
  0.0 817.7 jit_solution(15731884587893129483)
XLA Ops:
  6.5 0.0 copy-start
  6.5 0.0 all-gather.7.cloned.1.call-start
  6.5 0.7 all-gather.7.cloned.1.call-update
  7.3 0.0 all-gather.5.cloned.1.call-start
  7.3 0.7 all-gather.5.cloned.1.call-update
  8.0 0.0 all-gather.9.cloned.1.call-start
  8.7 4.0 copy.41
  12.7 0.0 copy-start.1
  12.7 0.0 copy-start.6
  12.7 2.1 convert_reduce_fusion
  14.8 0.1 copy-done.1
  14.9 0.6 fusion.5
  15.5 127.3 %all-gather.7.cloned.1.call-done = bf16[1,1024,1024]{2,1,0:T(8,128)(2,1)} async-done(((bf16[1,32,1024]{2,1,0:T(8,128)(2,1)}), bf16[1,1024,1024]{2,1,0:T(8,128)(2,1)}) %all-gather.7.cloned.1.call-update) | async-done | bytes 2097168 | tf_op jit(solution)/shard_map/all_gather | solution.py:48
  142.8 0.0 copy-done.6
  142.8 6.2 fusion.45
  149.1 148.2 %all-gather.5.cloned.1.call-done = bf16[1,1024,1024]{2,1,0:T(8,128)(2,1)} async-done(((bf16[1,32,1024]{2,1,0:T(8,128)(2,1)}), bf16[1,1024,1024]{2,1,0:T(8,128)(2,1)}) %all-gather.5.cloned.1.call-update) | async-done | bytes 2097168 | tf_op jit(solution)/shard_map/all_gather | solution.py:47
  297.2 6.8 convert_reduce_fusion.1
  304.0 0.0 copy-done.4
  304.0 1.5 fusion.61
  305.5 0.0 all-gather.9.cloned.1.call-update
  305.5 0.0 all-reduce.3.cloned.1.call-start
  305.6 49.3 %all-gather.9.cloned.1.call-done = f32[4,1024,128]{2,1,0:T(8,128)} async-done(((f32[1,1024,128]{2,1,0:T(8,128)}), f32[4,1024,128]{2,1,0:T(8,128)}) %all-gather.9.cloned.1.call-update) | async-done | bytes 2097168 | tf_op jit(solution)/shard_map/all_gather | solution.py:61
  354.9 2.9 copy.43
  357.8 0.0 all-reduce.3.cloned.1.call-update
  357.8 0.2 all-reduce.5.cloned.1.call-start
  358.1 7.6 fusion.24
  365.6 6.8 all-gather
  372.4 131.4 %psum.22 = f32[4,8,128]{2,0,1:T(4,128)S(1)} all-reduce(f32[4,8,128]{2,0,1:T(4,128)S(1)} %copy.48), channel_id=1, replica_groups=mesh['sec'=4,'pts'=32] {'pts'}, use_global_device_ids=true, to_apply=%region_4.5 | all-reduce | flops 4096 | bytes 32768 | tf_op jit(solution)/shard_map/psum | solution.py:64
  503.8 2.5 convolution_bitcast_fusion
  506.4 142.2 %all-reduce.3.cloned.1.call-done = f32[4,8,128,128]{2,3,0,1:T(8,128)} async-done(((f32[4,8,128,128]{2,3,0,1:T(8,128)}), f32[4,8,128,128]{2,3,0,1:T(8,128)}) %all-reduce.3.cloned.1.call-update) | async-done | bytes 2097168 | tf_op jit(solution)/shard_map/psum | solution.py:64
  648.5 9.9 %fusion = bf16[1024,8,128]{0,2,1:T(8,128)(2,1)S(1)} fusion(f32[4,8,128,128]{2,3,0,1:T(8,128)} %all-reduce.3.cloned.1.call-done, bf16[1024,8,128,1]{0,2,3,1:T(8,128)(2,1)} %bitcast.71, f32[4,1024,8]{1,0,2:T(4,128)S(1)} %convolution_bitcast_fusion), kind=kOutput, calls=%fused_computation.1 | convolution fusion | flops 6449790976 | bytes 6422528 | tf_op jit(solution)/shard_map/rhk,shkv->srhv/dot_general | solution.py:72
  658.5 0.0 copy-done
  658.5 0.0 copy-done.2
  658.5 2.6 fusion.58
  661.1 0.0 copy-start.3
  661.1 0.0 copy-start.5
  661.2 0.5 multiply_reduce_fusion
  661.6 1.4 copy-done.3
  663.0 0.0 copy-done.5
  663.1 2.0 fusion.25
  665.0 0.0 all-reduce.5.cloned.1.call-update
  665.1 0.3 reduce-scatter.2.cloned.1.call-start
  665.3 81.6 %all-reduce.5.cloned.1.call-done = bf16[1024,1024]{0,1:T(8,128)(2,1)} async-done(((bf16[1024,1024]{0,1:T(8,128)(2,1)}), bf16[1024,1024]{0,1:T(8,128)(2,1)}) %all-reduce.5.cloned.1.call-update) | async-done | bytes 2097168 | tf_op jit(solution)/shard_map/psum | solution.py:11
  746.9 11.3 %multiply_add_fusion = f32[1024,1024]{0,1:T(8,128)} fusion(f32[1024,1024]{0,1:T(8,128)} %copy-done.3, f32[]{:T(128)S(6)} %convert_element_type.62, bf16[1024,1024]{1,0:T(8,128)(2,1)} %param.19, bf16[1024,1024]{0,1:T(8,128)(2,1)} %all-reduce.5.cloned.1.call-done, bf16[1024,1024]{1,0:T(8,128)(2,1)} %param.18), kind=kOutput, calls=%fused_computation.34 | convolution fusion | flops 4306501632 | bytes 14680068 | tf_op jit(solution)/shard_map/dot_general | solution.py:90
  758.2 0.0 reduce-scatter.2.cloned.1.call-update
  758.2 50.3 %reduce-scatter.2.cloned.1.call-done = f32[1024,256]{0,1:T(8,128)} async-done(((f32[1024,1024]{0,1:T(8,128)}), f32[1024,256]{0,1:T(8,128)}) %reduce-scatter.2.cloned.1.call-update) | async-done | bytes 1048592 | tf_op jit(solution)/shard_map/reduce_scatter | solution.py:91
  808.5 1.3 convert_element_type.63
  809.8 1.0 copy.56
  (8 shorter events, 0.0 us)
Async XLA Ops:
  6.5 651.9 %copy-start = (bf16[1024,1024]{1,0:T(8,128)(2,1)S(1)}, bf16[1024,1024]{1,0:T(8,128)(2,1)}, u32[]{:S(2)}) copy-start(bf16[1024,1024]{1,0:T(8,128)(2,1)} %param.16) | copy-start | bytes 6291460
  6.5 136.3 %all-gather.7.cloned.1.call-start = ((), (), s32[]{:S(2)}) async-start(), calls=%async_computation.2 | async-start | bytes 2162688 | tf_op jit(solution)/shard_map/all_gather | solution.py:48
  7.3 290.0 %all-gather.5.cloned.1.call-start = ((), (), s32[]{:S(2)}) async-start(), calls=%async_computation.1 | async-start | bytes 2162688 | tf_op jit(solution)/shard_map/all_gather | solution.py:47
  8.0 346.9 %all-gather.9.cloned.1.call-start = ((), (), s32[]{:S(2)}) async-start(), calls=%async_computation.3 | async-start | bytes 2621440 | tf_op jit(solution)/shard_map/all_gather | solution.py:61
  12.7 2.2 copy-start.1
  12.7 130.2 %copy-start.6 = (f32[1,1024]{1,0:T(1,128)S(1)}, f32[1,1024]{1,0:T(1,128)}, u32[]{:S(2)}) copy-start(f32[1,1024]{1,0:T(1,128)} %param.12) | copy-start | bytes 12292
  297.2 6.8 copy-start.4
  305.5 343.0 %all-reduce.3.cloned.1.call-start = ((), (), s32[]{:S(2)}) async-start(), calls=%async_computation.4 | async-start | bytes 4194304 | tf_op jit(solution)/shard_map/psum | solution.py:64
  357.8 389.1 %all-reduce.5.cloned.1.call-start = ((), (), s32[]{:S(2)}) async-start(), calls=%async_computation.5 | async-start | bytes 4194304 | tf_op jit(solution)/shard_map/psum | solution.py:11
  648.5 10.0 %copy-start.2 = (bf16[1,1024,1024]{1,2,0:T(8,128)(2,1)S(1)}, bf16[1,1024,1024]{1,2,0:T(8,128)(2,1)}, u32[]{:S(2)}) copy-start(bf16[1,1024,1024]{1,2,0:T(8,128)(2,1)} %copy.41) | copy-start | bytes 6291460
  661.1 1.9 copy-start.3
  661.1 1.9 copy-start.5
  665.1 143.5 %reduce-scatter.2.cloned.1.call-start = ((), (), s32[]{:S(2)}) async-start(), calls=%async_computation.6 | async-start | bytes 5242880 | tf_op jit(solution)/shard_map/reduce_scatter | solution.py:91
Sparse Core Ops, SparseCore 0:
  9.0 133.8 all-gather.6
  144.5 152.6 all-gather.4
  305.7 49.2 all-gather.8
  357.9 290.5 all-reduce.2
  665.2 81.6 all-reduce.4
  758.3 50.1 reduce-scatter.1
where the time goes:
time: 818 us
  waiting for transfers between devices  600 us (73%)
  blocking collectives  138 us (17%)
  matrix products  48.4 us (6%)
  between operations  14.2 us (2%)
  local copies, waits for them, and re-layouts  9.38 us (1%)
    all_gather x1, waiting for transfers between devices, on_device(): lax.all_gather(key_weight, 'pts', axis=1, tiled=True)  148 us
    psum x1, waiting for transfers between devices, on_device(): state_matrices, totals = lax.psum((part_state, part_total), 'pts')  142 us
    psum x1, blocking collectives, on_device(): state_matrices, totals = lax.psum((part_state, part_total), 'pts')  131 us
    all_gather x1, waiting for transfers between devices, on_device(): lax.all_gather(value_weight, 'pts', axis=1, tiled=True)  127 us
    psum x1, waiting for transfers between devices, broadcast(): return lax.psum(jnp.where(mine, value, jnp.zeros_like(value)), axis)  81.6 us
    reduce_scatter x1, waiting for transfers between devices, on_device(): lax.psum_scatter(term, 'sec', scatter_dimension=1, tiled=True)  50.3 us
    all_gather x1, waiting for transfers between devices, on_device(): lax.all_gather(local_state[None], 'sec', axis=0, tiled=True)  49.3 us
  transfers between devices with their start and end apart: 6, of which 6 were waited for; matrix products, arithmetic and copies ran while one was open for 3% of the time, Pallas kernels for 0%

commit v1 on v0

--- a/solution.py
+++ b/solution.py
@@ -8,7 +8,7 @@
 
 def broadcast(value, axis, root):
     mine = lax.axis_index(axis) == root
-    return lax.psum(jnp.where(mine, value, jnp.zeros_like(value)), axis)
+    return jnp.sum(lax.all_gather(jnp.where(mine, value, jnp.zeros_like(value)), axis), axis=0)
 
 
 def layer_normalizer(values, gain):

time: 818 us -> 850 us (1.039)
  local copies, waits for them, and re-layouts: 9.38 us -> 23.9 us
  other arithmetic: 6.49 us -> 19.4 us
    all_gather x0 -> x1, waiting for transfers between devices: none -> 85.2 us  [broadcast(): lax.all_gather(jnp.where(mine, value, jnp.zeros_like(value)), axis)]
    psum x1 -> x0, waiting for transfers between devices: 81.6 us -> none  [broadcast(): return lax.psum(jnp.where(mine, value, jnp.zeros_like(value)), axis)]
    all_gather x0 -> x1, local copies, waits for them, and re-layouts: none -> 14.6 us  [broadcast(): lax.all_gather(jnp.where(mine, value, jnp.zeros_like(value)), axis)]
    reduce_sum x0 -> x1, other arithmetic: none -> 12.9 us  [broadcast(): jnp.sum(lax.all_gather(jnp.where(mine, value, jnp.zeros_like(value)), axi...]
where the time goes in v1:
time: 850 us; the launch traced here: 849 us
  waiting for transfers between devices  604 us (71%)
  blocking collectives  138 us (16%)
  matrix products  48.4 us (6%)
  local copies, waits for them, and re-layouts  23.9 us (3%)
  other arithmetic  19.4 us (2%)
  between operations  14.2 us (2%)
    all_gather x1, waiting for transfers between devices, on_device(): lax.all_gather(key_weight, 'pts', axis=1, tiled=True)  148 us
    psum x1, waiting for transfers between devices, on_device(): state_matrices, totals = lax.psum((part_state, part_total), 'pts')  142 us
    psum x1, blocking collectives, on_device(): state_matrices, totals = lax.psum((part_state, part_total), 'pts')  131 us
    all_gather x1, waiting for transfers between devices, on_device(): lax.all_gather(value_weight, 'pts', axis=1, tiled=True)  127 us
    all_gather x1, waiting for transfers between devices, broadcast(): lax.all_gather(jnp.where(mine, value, jnp.zeros_like(value)), axis)  85.2 us
    reduce_scatter x1, waiting for transfers between devices, on_device(): lax.psum_scatter(term, 'sec', scatter_dimension=1, tiled=True)  50.4 us
    all_gather x1, waiting for transfers between devices, on_device(): lax.all_gather(local_state[None], 'sec', axis=0, tiled=True)  49.3 us
  transfers between devices with their start and end apart: 6, of which 6 were waited for; matrix products, arithmetic and copies ran while one was open for 3% of the time, Pallas kernels for 0%

profile of v1, /device:TPU:1, one launch (start us, length us, event | category | flops | bytes accessed | tf_op | source)
XLA Modules:
  0.0 848.8 jit_solution(16009192727181119187)
XLA Ops:
  6.5 0.0 copy-start
  6.5 0.0 all-gather.9.cloned.1.call-start
  6.5 0.7 all-gather.9.cloned.1.call-update
  7.3 0.0 all-gather.7.cloned.1.call-start
  7.3 0.7 all-gather.7.cloned.1.call-update
  8.0 0.0 all-gather.11.cloned.1.call-start
  8.7 4.0 copy.41
  12.7 0.0 copy-start.6
  12.7 2.1 convert_reduce_fusion
  14.8 0.1 copy-done.1
  14.9 0.6 fusion.5
  15.5 127.3 %all-gather.9.cloned.1.call-done = bf16[1,1024,1024]{2,1,0:T(8,128)(2,1)} async-done(((bf16[1,32,1024]{2,1,0:T(8,128)(2,1)}), bf16[1,1024,1024]{2,1,0:T(8,128)(2,1)}) %all-gather.9.cloned.1.call-update) | async-done | bytes 2097168 | tf_op jit(solution)/shard_map/all_gather | solution.py:48
  142.8 0.0 copy-done.6
  142.8 6.2 fusion.45
  149.1 148.2 %all-gather.7.cloned.1.call-done = bf16[1,1024,1024]{2,1,0:T(8,128)(2,1)} async-done(((bf16[1,32,1024]{2,1,0:T(8,128)(2,1)}), bf16[1,1024,1024]{2,1,0:T(8,128)(2,1)}) %all-gather.7.cloned.1.call-update) | async-done | bytes 2097168 | tf_op jit(solution)/shard_map/all_gather | solution.py:47
  297.2 6.8 convert_reduce_fusion.1
  304.0 0.0 copy-done.4
  304.0 1.5 fusion.61
  305.5 0.0 all-gather.11.cloned.1.call-update
  305.5 0.0 all-reduce.2.cloned.1.call-start
  305.6 49.3 %all-gather.11.cloned.1.call-done = f32[4,1024,128]{2,1,0:T(8,128)} async-done(((f32[1,1024,128]{2,1,0:T(8,128)}), f32[4,1024,128]{2,1,0:T(8,128)}) %all-gather.11.cloned.1.call-update) | async-done | bytes 2097168 | tf_op jit(solution)/shard_map/all_gather | solution.py:61
  354.9 2.9 copy.43
  357.8 0.0 all-reduce.2.cloned.1.call-update
  357.8 0.2 all-gather.13.cloned.1.call-start
  358.1 7.6 fusion.24
  365.6 6.8 all-gather
  372.4 131.4 %psum.15 = f32[4,8,128]{2,0,1:T(4,128)S(1)} all-reduce(f32[4,8,128]{2,0,1:T(4,128)S(1)} %copy.48), channel_id=1, replica_groups=mesh['sec'=4,'pts'=32] {'pts'}, use_global_device_ids=true, to_apply=%region_4.5 | all-reduce | flops 4096 | bytes 32768 | tf_op jit(solution)/shard_map/psum | solution.py:64
  503.8 2.5 convolution_bitcast_fusion
  506.4 142.2 %all-reduce.2.cloned.1.call-done = f32[4,8,128,128]{2,3,0,1:T(8,128)} async-done(((f32[4,8,128,128]{2,3,0,1:T(8,128)}), f32[4,8,128,128]{2,3,0,1:T(8,128)}) %all-reduce.2.cloned.1.call-update) | async-done | bytes 2097168 | tf_op jit(solution)/shard_map/psum | solution.py:64
  648.5 9.9 %fusion = bf16[1024,8,128]{0,2,1:T(8,128)(2,1)S(1)} fusion(f32[4,8,128,128]{2,3,0,1:T(8,128)} %all-reduce.2.cloned.1.call-done, bf16[1024,8,128,1]{0,2,3,1:T(8,128)(2,1)} %bitcast.73, f32[4,1024,8]{1,0,2:T(4,128)S(1)} %convolution_bitcast_fusion), kind=kOutput, calls=%fused_computation.1 | convolution fusion | flops 6449790976 | bytes 6422528 | tf_op jit(solution)/shard_map/rhk,shkv->srhv/dot_general | solution.py:72
  658.5 0.0 copy-done
  658.5 0.0 copy-done.2
  658.5 2.6 fusion.58
  661.1 0.0 copy-start.3
  661.1 0.0 copy-start.5
  661.2 0.5 multiply_reduce_fusion
  661.6 1.4 copy-done.3
  663.0 2.0 fusion.25
  665.1 0.0 all-gather.13.cloned.1.call-update
  665.1 0.3 reduce-scatter.2.cloned.1.call-start
  665.4 85.2 %all-gather.13.cloned.1.call-done = bf16[4096,1024]{0,1:T(8,128)(2,1)} async-done(((bf16[1024,1024]{0,1:T(8,128)(2,1)}), bf16[4096,1024]{0,1:T(8,128)(2,1)}) %all-gather.13.cloned.1.call-update) | async-done | bytes 8388624 | tf_op jit(solution)/shard_map/all_gather | solution.py:11
  750.6 14.6 %reshape.96 = bf16[4,1024,1024]{1,0,2:T(4,128)(2,1)} reshape(bf16[4096,1024]{0,1:T(8,128)(2,1)} %all-gather.13.cloned.1.call-done) | data formatting | bytes 16777216 | tf_op jit(solution)/shard_map/all_gather | solution.py:11
  765.1 12.9 %reduce_sum.72 = bf16[1024,1024]{0,1:T(8,128)(2,1)} reduce(bf16[4,1024,1024]{1,0,2:T(4,128)(2,1)} %reshape.96, bf16[]{:T(256)} %constant.31.clone.1), dimensions={0}, to_apply=%region_8.9 | reduce | flops 3145728 | bytes 10485762 | tf_op jit(solution)/shard_map/reduce_sum | solution.py:11
  778.0 11.3 %multiply_add_fusion = f32[1024,1024]{0,1:T(8,128)} fusion(f32[1024,1024]{0,1:T(8,128)} %copy-done.3, f32[]{:T(128)S(6)} %convert_element_type.64, bf16[1024,1024]{1,0:T(8,128)(2,1)} %param.19, bf16[1024,1024]{0,1:T(8,128)(2,1)} %reduce_sum.72, bf16[1024,1024]{1,0:T(8,128)(2,1)} %param.18), kind=kOutput, calls=%fused_computation.34 | convolution fusion | flops 4306501632 | bytes 14680068 | tf_op jit(solution)/shard_map/dot_general | solution.py:90
  789.3 0.0 reduce-scatter.2.cloned.1.call-update
  789.3 50.4 %reduce-scatter.2.cloned.1.call-done = f32[1024,256]{0,1:T(8,128)} async-done(((f32[1024,1024]{0,1:T(8,128)}), f32[1024,256]{0,1:T(8,128)}) %reduce-scatter.2.cloned.1.call-update) | async-done | bytes 1048592 | tf_op jit(solution)/shard_map/reduce_scatter | solution.py:91
  839.7 1.3 convert_element_type.65
  841.0 1.0 copy.56
  (10 shorter events, 0.0 us)
Async XLA Ops:
  6.5 651.9 %copy-start = (bf16[1024,1024]{1,0:T(8,128)(2,1)S(1)}, bf16[1024,1024]{1,0:T(8,128)(2,1)}, u32[]{:S(2)}) copy-start(bf16[1024,1024]{1,0:T(8,128)(2,1)} %param.16) | copy-start | bytes 6291460
  6.5 136.3 %all-gather.9.cloned.1.call-start = ((), (), s32[]{:S(2)}) async-start(), calls=%async_computation.2 | async-start | bytes 2162688 | tf_op jit(solution)/shard_map/all_gather | solution.py:48
  7.3 290.0 %all-gather.7.cloned.1.call-start = ((), (), s32[]{:S(2)}) async-start(), calls=%async_computation.1 | async-start | bytes 2162688 | tf_op jit(solution)/shard_map/all_gather | solution.py:47
  8.0 346.9 %all-gather.11.cloned.1.call-start = ((), (), s32[]{:S(2)}) async-start(), calls=%async_computation.3 | async-start | bytes 2621440 | tf_op jit(solution)/shard_map/all_gather | solution.py:61
  12.7 2.2 copy-start.1
  12.7 130.2 %copy-start.6 = (f32[1,1024]{1,0:T(1,128)S(1)}, f32[1,1024]{1,0:T(1,128)}, u32[]{:S(2)}) copy-start(f32[1,1024]{1,0:T(1,128)} %param.12) | copy-start | bytes 12292
  297.2 6.8 copy-start.4
  305.5 343.0 %all-reduce.2.cloned.1.call-start = ((), (), s32[]{:S(2)}) async-start(), calls=%async_computation.4 | async-start | bytes 4194304 | tf_op jit(solution)/shard_map/psum | solution.py:64
  357.8 392.8 %all-gather.13.cloned.1.call-start = ((), (), s32[]{:S(2)}) async-start(), calls=%async_computation.6 | async-start | bytes 10485760 | tf_op jit(solution)/shard_map/all_gather | solution.py:11
  648.5 10.0 %copy-start.2 = (bf16[1,1024,1024]{1,2,0:T(8,128)(2,1)S(1)}, bf16[1,1024,1024]{1,2,0:T(8,128)(2,1)}, u32[]{:S(2)}) copy-start(bf16[1,1024,1024]{1,2,0:T(8,128)(2,1)} %copy.41) | copy-start | bytes 6291460
  661.1 1.9 copy-start.3
  661.1 1.9 copy-start.5
  665.1 174.6 %reduce-scatter.2.cloned.1.call-start = ((), (), s32[]{:S(2)}) async-start(), calls=%async_computation.5 | async-start | bytes 5242880 | tf_op jit(solution)/shard_map/reduce_scatter | solution.py:91
Sparse Core Ops, SparseCore 0:
  9.0 133.8 all-gather.8
  144.5 152.6 all-gather.6
  305.7 49.2 all-gather.10
  357.9 290.5 all-reduce.1
  665.2 85.2 all-gather.12
  789.4 50.2 reduce-scatter.1
